TPU v7x, 128 devices: a whole 4x4x4 slice. The times are simulated.
128 devices in a mesh: req: 8 (over z, core), shard: 16 (over x, y).
Axes of the slice: x: 4, y: 4, z: 4, core: 2. Of those that a mesh axis runs over, the one named last changes fastest.
Arguments:
- hidden_states: bfloat16 [16384, 1536], P(('req', 'shard')), may hold values from -6 to 6
- attn_gain: float32 [1536], replicated, may hold values from 0.5 to 1.5
- w_qkv: bfloat16 [1536, 2560], replicated, may hold values from -0.15625 to 0.15625
- w_out: bfloat16 [1536, 1536], replicated, may hold values from -0.15625 to 0.15625
- kv_cache: bfloat16 [8, 4096, 1024], P('req', 'shard'), may hold values from -80 to 80, as said below
- cached_len: int32 [8], P('req'), may hold values from 128 to 4096, as said below
- ffn_gain: float32 [1536], replicated, may hold values from 0.5 to 1.5
- w_router: bfloat16 [1536, 40], replicated, may hold values from -0.15625 to 0.15625
- expert_ids: int32 [16384, 8], P(('req', 'shard')), may hold values from 0 to 39, all different within a row; in each aligned block of 128 rows (0 to 127, 128 to 255, ...) at most 32 rows name the same one
- w_gate: bfloat16 [40, 512, 1536], P('req', 'shard'), may hold values from -0.15625 to 0.15625
- w_up: bfloat16 [40, 512, 1536], P('req', 'shard'), may hold values from -0.15625 to 0.15625
- w_down: bfloat16 [40, 512, 1536], P('req', 'shard'), may hold values from -0.25 to 0.25
Outputs:
- layer_out: bfloat16 [16384, 1536], P(('req', 'shard'))
Inputs may be any that keep to these rules, and one draw needn't show every extreme that they name: `cached_len`: each request's length is drawn either between 128 and 512 or between 3072 and 4096; some request has exactly 4096. `expert_ids`: among the 128 rows of one device no expert is named by more than 32 rows. `kv_cache`: cached keys and values, already rotated.
All inputs are finite; a program needn't handle non-finite values.
Results may differ from a plain program's by a relative error of at most 0.025.
Values may be sent and summed in bfloat16 or wider, within the bound.
No kernel may reach another device: no remote copies, remote signals or barrier semaphores. Data moves between devices by JAX's collectives and lax.ppermute only.
A program may use at most 192 MiB of HBM per device.

v0:
```python
import math
import jax
import jax.numpy as jnp
from jax import lax
from jax.sharding import PartitionSpec as P

D = 1536
HEADS = 24
KVH = 8
HD = 64
TOP = 8
EPSILON = 1e-05
NEG_FILL = -1e30
FAR_LIMIT = 1 << 30


def rms_scale(values, gain):
    floats = values.astype(jnp.float32)
    inverse = lax.rsqrt(jnp.mean(floats * floats, axis=-1, keepdims=True) + EPSILON)
    return (floats * inverse * gain).astype(jnp.bfloat16)


def rotate(values, positions):
    half_dim = values.shape[-1] // 2
    freqs = jnp.power(10000.0, -jnp.arange(half_dim, dtype=jnp.float32) / half_dim)
    angles = positions.astype(jnp.float32)[:, None] * freqs[None, :]
    cosine = jnp.cos(angles)[:, None, :]
    sine = jnp.sin(angles)[:, None, :]
    first = values[..., :half_dim]
    second = values[..., half_dim:]
    return jnp.concatenate(
        [first * cosine - second * sine, second * cosine + first * sine], axis=-1
    )


def empty_state(rows):
    groups = HEADS // KVH
    return (
        jnp.full((rows, KVH, groups), NEG_FILL, jnp.float32),
        jnp.zeros((rows, KVH, groups), jnp.float32),
        jnp.zeros((rows, KVH, groups, HD), jnp.float32),
    )


def attend_block(state, queries, query_pos, block, key_pos, key_limit):
    max_run, total, accum = state
    rows = block.shape[0]
    keys = block[:, : KVH * HD].reshape(rows, KVH, HD)
    values = block[:, KVH * HD :].reshape(rows, KVH, HD)
    scores = jnp.einsum(
        "tgqd,rgd->tgqr", queries, keys, preferred_element_type=jnp.float32
    ) * HD ** (-0.5)
    allowed = (key_pos[None, :] <= query_pos[:, None]) & (key_pos < key_limit)[None, :]
    allowed = allowed[:, None, None, :]
    block_max = jnp.max(jnp.where(allowed, scores, NEG_FILL), axis=-1)
    new_max = jnp.maximum(max_run, block_max)
    weights = jnp.where(allowed, jnp.exp(scores - new_max[..., None]), 0.0)
    factor = jnp.exp(max_run - new_max)
    total = total * factor + jnp.sum(weights, axis=-1)
    accum = accum * factor[..., None] + jnp.einsum(
        "tgqr,rgd->tgqd", weights.astype(jnp.bfloat16), values, preferred_element_type=jnp.float32
    )
    return (new_max, total, accum)


def fold_rows(state, queries, query_pos, piece, key_pos, key_limit):
    rows = piece.shape[0]
    step_rows = math.gcd(rows, 512)
    count = rows // step_rows
    blocks = piece.reshape(count, step_rows, piece.shape[1])
    positions = key_pos.reshape(count, step_rows)

    def advance(carry, item):
        return (attend_block(carry, queries, query_pos, item[0], item[1], key_limit), None)

    state, _ = lax.scan(advance, state, (blocks, positions))
    return state


def local(
    hidden_states,
    attn_gain,
    w_qkv,
    w_out,
    kv_cache,
    cached_len,
    ffn_gain,
    w_router,
    expert_ids,
    w_gate,
    w_up,
    w_down,
):
    groups = HEADS // KVH
    tok_rows = hidden_states.shape[0]
    shard_pos = lax.axis_index("shard")
    length = cached_len[0]
    normed = rms_scale(hidden_states, attn_gain)
    qkv = jnp.dot(normed, w_qkv, preferred_element_type=jnp.float32)
    positions = length + shard_pos * tok_rows + jnp.arange(tok_rows, dtype=jnp.int32)
    queries = rotate(qkv[:, : HEADS * HD].reshape(tok_rows, HEADS, HD), positions).astype(
        jnp.bfloat16
    )
    new_keys = rotate(
        qkv[:, HEADS * HD : (HEADS + KVH) * HD].reshape(tok_rows, KVH, HD), positions
    ).astype(jnp.bfloat16)
    new_values = qkv[:, (HEADS + KVH) * HD :].astype(jnp.bfloat16)
    new_kv = jnp.concatenate([new_keys.reshape(tok_rows, KVH * HD), new_values], axis=1)
    cache_local = kv_cache[0]
    query_heads = queries.reshape(tok_rows, KVH, groups, HD)
    piece = lax.all_gather(cache_local, "shard", axis=0, tiled=True)
    key_pos = jnp.arange(piece.shape[0], dtype=jnp.int32)
    state = fold_rows(empty_state(tok_rows), query_heads, positions, piece, key_pos, length)
    piece = lax.all_gather(new_kv, "shard", axis=0, tiled=True)
    key_pos = length + jnp.arange(piece.shape[0], dtype=jnp.int32)
    max_run, total, accum = fold_rows(state, query_heads, positions, piece, key_pos, FAR_LIMIT)
    attended = (accum / total[..., None]).astype(jnp.bfloat16)
    attended = attended.reshape(tok_rows, HEADS * HD)
    mid = (
        hidden_states.astype(jnp.float32)
        + jnp.dot(attended, w_out, preferred_element_type=jnp.float32)
    ).astype(jnp.bfloat16)
    normed2 = rms_scale(mid, ffn_gain)
    group_count = lax.axis_size("req")
    local_experts = w_gate.shape[0]
    expert_count = local_experts * group_count
    capacity = min(tok_rows, 5 * tok_rows * TOP // (4 * expert_count))
    logits = jnp.dot(normed2, w_router, preferred_element_type=jnp.float32)
    picked = expert_ids[:, :, None] == jnp.arange(expert_count, dtype=jnp.int32)[None, None, :]
    chosen = jnp.sum(jnp.where(picked, logits[:, None, :], 0.0), axis=-1)
    gates = jax.nn.softmax(chosen, axis=-1)
    flat_hot = picked.reshape(tok_rows * TOP, expert_count).astype(jnp.int32)
    ranks = jnp.cumsum(flat_hot, axis=0) - flat_hot
    slot_rank = jnp.sum(ranks * flat_hot, axis=-1)
    slots = expert_ids.reshape(-1) * capacity + slot_rank
    slot_table = (
        slots.reshape(tok_rows, TOP)[:, :, None]
        == jnp.arange(expert_count * capacity, dtype=jnp.int32)[None, None, :]
    )
    placing = jnp.any(slot_table, axis=1).astype(jnp.bfloat16)
    outgoing = jnp.einsum("ts,td->sd", placing, normed2, preferred_element_type=jnp.float32).astype(
        jnp.bfloat16
    )
    outgoing = outgoing.reshape(group_count, local_experts, capacity, D)
    arrived = lax.all_to_all(outgoing, "req", split_axis=0, concat_axis=0, tiled=True)
    weights = jnp.concatenate([w_gate, w_up, w_down], axis=-1)
    weights = lax.all_gather(weights, "shard", axis=1, tiled=True)
    gate_piece = weights[..., :D]
    up_piece = weights[..., D : 2 * D]
    down_piece = weights[..., 2 * D :]
    gate = jnp.einsum("sjcd,jhd->sjch", arrived, gate_piece, preferred_element_type=jnp.float32)
    upper = jnp.einsum("sjcd,jhd->sjch", arrived, up_piece, preferred_element_type=jnp.float32)
    inner = (jax.nn.silu(gate) * upper).astype(jnp.bfloat16)
    summed = jnp.einsum("sjch,jhd->sjcd", inner, down_piece, preferred_element_type=jnp.float32)
    returned = lax.all_to_all(
        summed.astype(jnp.bfloat16), "req", split_axis=0, concat_axis=0, tiled=True
    )
    returned = returned.reshape(expert_count * capacity, D)
    expert_rows = returned[slots].reshape(tok_rows, TOP, D)
    mixture = jnp.sum(gates[:, :, None] * expert_rows.astype(jnp.float32), axis=1)
    return (mid.astype(jnp.float32) + mixture).astype(jnp.bfloat16)


def solution(mesh):
    return jax.shard_map(
        local,
        mesh=mesh,
        in_specs=(
            P(("req", "shard"), None),
            P(),
            P(),
            P(),
            P("req", "shard", None),
            P("req"),
            P(),
            P(),
            P(("req", "shard"), None),
            P("req", "shard", None),
            P("req", "shard", None),
            P("req", "shard", None),
        ),
        out_specs=P(("req", "shard"), None),
        check_vma=False,
    )
```

profile of v0, /device:TPU:1, one launch (start us, length us, event | category | flops | bytes accessed | tf_op | source)
XLA Modules:
  0.0 382.5 jit_solution(826455171912664360)
XLA Ops:
  8.5 4.7 %fusion.60 = f32[128,2560]{1,0:T(8,128)S(1)} fusion(bf16[1536,2560]{1,0:T(8,128)(2,1)} %param.18, bf16[128,1536]{1,0:T(8,128)(2,1)} %param.16, f32[1536]{0:T(1024)} %param.17, f32[128]{0:T(128)S(1)} %add_rsqrt_fusion.1), kind=kOutput, calls=%fused_computation.82 | convolution fusion | flops 1007419392 | bytes 9574912 | tf_op jit(solution)/shard_map/dot_general | solution.py:99
  15.3 2.3 pad_maximum_fusion
  18.0 11.3 %reduce-window.6 = s32[40,8,128]{2,1,0:T(8,128)S(1)} reduce-window(s32[40,8,128]{2,1,0:T(8,128)S(1)} %fusion.67, s32[]{:T(128)} %copy.121), window={size=1x1x128 pad=0_0x0_0x127_0}, to_apply=%region_13.14 | reduce-window | flops 5201920 | bytes 327684 | tf_op jit(solution)/shard_map/reduce-window
  30.3 1.6 fusion.41
  32.0 51.2 %all-gather.9.cloned.1.call-done = bf16[1,4096,1024]{2,1,0:T(8,128)(2,1)} async-done(((bf16[1,256,1024]{2,1,0:T(8,128)(2,1)}), bf16[1,4096,1024]{2,1,0:T(8,128)(2,1)}) %all-gather.9.cloned.1.call-update) | async-done | bytes 8388624 | tf_op jit(solution)/shard_map/all_gather | solution.py:111
  83.2 60.8 %while.31 = (s32[]{:T(128)}, f32[128,8,3]{0,2,1:T(4,128)S(1)}, f32[128,8,3]{0,2,1:T(4,128)S(1)}, f32[128,8,3,64]{0,3,2,1:T(8,128)}, s32[8,512]{1,0:T(8,128)S(1)}...) while((s32[]{:T(128)}, f32[128,8,3]{0,2,1:T(4,128)S(1)}, ...), condition=%wide.region_4.5_spmd.clone, body=%wide.region_1.4_spmd.clone.sunk | while | flops 420691584 | bytes 34939080 | solution.py:76
  88.5 1.4 fusion.119
  111.2 1.4 fusion.119
  118.8 1.4 fusion.119
  126.4 1.4 fusion.119
  134.1 1.4 fusion.119
  141.7 1.4 fusion.119
  144.0 28.0 %while.30 = (s32[]{:T(128)}, f32[128,8,3]{0,2,1:T(4,128)S(1)}, f32[128,8,3]{0,2,1:T(4,128)S(1)}, f32[128,8,3,64]{0,3,2,1:T(8,128)}, s32[4,512]{1,0:T(4,128)S(1)}...) while((s32[]{:T(128)}, f32[128,8,3]{0,2,1:T(4,128)S(1)}, ...), condition=%wide.region_8.9_spmd.clone, body=%wide.region_5.8_spmd.clone.sunk | while | flops 420485760 | bytes 34939048 | solution.py:76
  151.2 1.5 constant_dynamic-slice_fusion.8
  173.3 3.2 multiply_reduce_fusion
  177.8 50.9 %all_to_all.10 = bf16[8,5,32,1536]{3,2,1,0:T(8,128)(2,1)} all-to-all(bf16[8,5,32,1536]{3,2,1,0:T(8,128)(2,1)S(1)} %bitcast.209), channel_id=1, replica_groups=mesh['req'=8,'shard'=16] {'req'}, dimensions={0} | all-to-all | bytes 7864320 | tf_op jit(solution)/shard_map/all_to_all | solution.py:145
  228.7 55.6 %all-gather.7.cloned.1.call-done = bf16[5,512,4608]{2,1,0:T(8,128)(2,1)} async-done(((bf16[5,32,4608]{2,1,0:T(8,128)(2,1)}), bf16[5,512,4608]{2,1,0:T(8,128)(2,1)}) %all-gather.7.cloned.1.call-update) | async-done | bytes 23592976 | tf_op jit(solution)/shard_map/all_gather | solution.py:147
  284.2 8.1 %fusion.38 = f32[5,512,8,32]{1,3,2,0:T(8,128)} fusion(bf16[5,512,4608]{2,1,0:T(8,128)(2,1)} %all-gather.7.cloned.1.call-done, bf16[8,5,32,1536]{3,2,1,0:T(8,128)(2,1)} %all_to_all.10), kind=kOutput, calls=%fused_computation.49 | convolution fusion | flops 2013265920 | bytes 14417920 | tf_op jit(solution)/shard_map/sjcd,jhd->sjch/dot_general | solution.py:151
  292.3 12.6 %fusion.43 = bf16[8,5,32,1536]{3,2,0,1:T(8,128)(2,1)} fusion(bf16[5,512,4608]{2,1,0:T(8,128)(2,1)} %all-gather.7.cloned.1.call-done, f32[5,512,8,32]{1,3,2,0:T(8,128)} %fusion.38, bf16[8,5,32,1536]{3,2,1,0:T(8,128)(2,1)} %all_to_all.10), kind=kOutput, calls=%fused_computation.58 | convolution fusion | flops 4032430080 | bytes 26214400 | tf_op jit(solution)/shard_map/sjch,jhd->sjcd/dot_general | solution.py:154
  304.9 4.5 %copy.70 = bf16[8,5,32,1536]{3,2,1,0:T(8,128)(2,1)} copy(bf16[8,5,32,1536]{3,2,0,1:T(8,128)(2,1)} %fusion.43) | data formatting | bytes 7864320 | tf_op jit(solution)/shard_map/convert_element_type | solution.py:156
  309.3 5.3 %all-to-all-start.1 = ((bf16[8,5,32,1536]{3,2,1,0:T(8,128)(2,1)}), bf16[8,5,32,1536]{3,2,1,0:T(8,128)(2,1)}, u32[]{:S(2)}, u32[]{:S(2)}) async-start(bf16[8,5,32,1536]{3,2,1,0:T(8,128)(2,1)} %copy.70), calls=%async_computation.1 | async-start | bytes 7864320 | tf_op jit(solution)/shard_map/all_to_all | solution.py:155
  315.2 45.3 %all-to-all-done.1 = bf16[8,5,32,1536]{3,2,1,0:T(8,128)(2,1)} async-done(((bf16[8,5,32,1536]{3,2,1,0:T(8,128)(2,1)}), bf16[8,5,32,1536]{3,2,1,0:T(8,128)(2,1)}, u32[]{:S(2)}, u32[]{:S(2)}) %all-to-all-start.1) | async-done | bytes 3932192 | tf_op jit(solution)/shard_map/all_to_all | solution.py:155
  360.5 9.9 %gather_fusion = bf16[1024,1536]{1,0:T(8,128)(2,1)} fusion(bf16[1280,1536]{1,0:T(8,128)(2,1)} %bitcast.21, s32[1024]{0:T(1024)S(1)} %broadcast_clamp_fusion), kind=kCustom, calls=%fused_computation | custom fusion | bytes 6295552 | tf_op jit(solution)/shard_map/gather | solution.py:159
  370.4 4.7 %fusion.40 = f32[128,1536]{1,0:T(8,128)S(1)} fusion(bf16[1024,1536]{1,0:T(8,128)(2,1)} %gather_fusion, f32[128,8]{1,0:T(8,128)S(1)} %copy.62), kind=kLoop, calls=%fused_computation.54 | loop fusion | flops 4521984 | bytes 3936256 | tf_op jit(solution)/shard_map/reduce_sum | solution.py:160
  (251 shorter events, 86.4 us)
Async XLA Ops:
  6.5 308.2 %copy-start = (bf16[1536,40]{0,1:T(8,128)(2,1)S(1)}, bf16[1536,40]{0,1:T(8,128)(2,1)}, u32[]{:S(2)}) copy-start(bf16[1536,40]{0,1:T(8,128)(2,1)} %param.23) | copy-start | bytes 368644
  6.5 76.7 %all-gather.9.cloned.1.call-start = ((), (), s32[]{:S(2)}) async-start(), calls=%async_computation.4 | async-start | bytes 8912896 | tf_op jit(solution)/shard_map/all_gather | solution.py:111
  7.3 136.8 %all-gather.5.cloned.1.call-start = ((), (), s32[]{:S(2)}) async-start(), calls=%async_computation.2 | async-start | bytes 4456448 | tf_op jit(solution)/shard_map/all_gather | solution.py:114
  8.5 6.8 %copy-start.6 = (bf16[5,32,1536]{2,1,0:T(8,128)(2,1)S(1)}, bf16[5,32,1536]{2,1,0:T(8,128)(2,1)}, u32[]{:S(2)}) copy-start(bf16[5,32,1536]{2,1,0:T(8,128)(2,1)} %param.27) | copy-start | bytes 1474564
  8.5 6.8 %copy-start.7 = (bf16[5,32,1536]{2,1,0:T(8,128)(2,1)S(1)}, bf16[5,32,1536]{2,1,0:T(8,128)(2,1)}, u32[]{:S(2)}) copy-start(bf16[5,32,1536]{2,1,0:T(8,128)(2,1)} %param.26) | copy-start | bytes 1474564
  13.2 4.4 %copy-start.9 = (s32[128,8]{0,1:T(8,128)S(1)}, s32[128,8]{0,1:T(8,128)}, u32[]{:S(2)}) copy-start(s32[128,8]{0,1:T(8,128)} %param.24) | copy-start | bytes 12292
  15.2 269.0 %all-gather.7.cloned.1.call-start = ((), (), s32[]{:S(2)}) async-start(), calls=%async_computation.3 | async-start | bytes 25067520 | tf_op jit(solution)/shard_map/all_gather | solution.py:147
  86.0 2.4 copy-start.2
  89.9 0.9 copy-start.3
  93.6 2.4 copy-start.2
  97.5 0.9 copy-start.3
  101.2 2.4 copy-start.2
  108.8 2.4 copy-start.2
  116.4 2.4 copy-start.2
  124.0 2.4 copy-start.2
  131.7 2.4 copy-start.2
  139.2 2.4 copy-start.2
  144.0 29.2 %copy-start.1 = (bf16[128,1536]{1,0:T(8,128)(2,1)S(1)}, bf16[128,1536]{1,0:T(8,128)(2,1)}, u32[]{:S(2)}) copy-start(bf16[128,1536]{1,0:T(8,128)(2,1)} %param.16) | copy-start | bytes 1179652
  146.2 2.4 copy-start.4
  153.3 2.4 copy-start.4
  160.3 2.4 copy-start.4
  167.2 2.4 copy-start.4
  172.0 4.5 %copy-start.8 = (f32[1536]{0:T(1024)S(1)}, f32[1536]{0:T(1024)}, u32[]{:S(2)}) copy-start(f32[1536]{0:T(1024)} %param.22) | copy-start | bytes 18436
  309.3 51.2 %all-to-all-start.1 = ((bf16[8,5,32,1536]{3,2,1,0:T(8,128)(2,1)}), bf16[8,5,32,1536]{3,2,1,0:T(8,128)(2,1)}, u32[]{:S(2)}, u32[]{:S(2)}) async-start(bf16[8,5,32,1536]{3,2,1,0:T(8,128)(2,1)} %copy.70), calls=%async_computation.1 | async-start | bytes 7864320 | tf_op jit(solution)/shard_map/all_to_all | solution.py:155
  (10 other events, 9.1 us)
Sparse Core Ops, SparseCore 0:
  9.5 73.6 all-gather.8
  85.4 51.0 all-gather.4
  138.6 145.6 all-gather.6
where the time goes:
time: 384 us; the launch traced here: 383 us
  waiting for transfers between devices  153 us (40%)
  matrix products  60.4 us (16%)
  blocking collectives  50.9 us (13%)
  local copies, waits for them, and re-layouts  49.9 us (13%)
  other arithmetic  48.2 us (13%)
  between operations  14.1 us (4%)
  starting transfers between devices  5.34 us (1%)
    all_gather x1, waiting for transfers between devices, local(): weights = lax.all_gather(weights, 'shard', axis=1, tiled=True)  55.6 us
    all_gather x1, waiting for transfers between devices, local(): piece = lax.all_gather(cache_local, 'shard', axis=0, tiled=True)  51.2 us
    all_to_all x1, blocking collectives, local(): lax.all_to_all(outgoing, 'req', split_axis=0, concat_axis=0, tiled=True)  50.9 us
    all_to_all x1, waiting for transfers between devices, local(): lax.all_to_all(summed.astype(jnp.bfloat16), 'req', split_axis=0, concat_a...  45.3 us
    dynamic_slice x24, local copies, waits for them, and re-layouts, fold_rows(): state, _ = lax.scan(advance, state, (blocks, positions))  22.4 us
    dot_general x12, matrix products, attend_block(): jnp.einsum('tgqr,rgd->tgqd', weights.astype(jnp.bfloat16), values, prefer...  17.3 us
    reduce_sum x12, other arithmetic, attend_block(): total = total * factor + jnp.sum(weights, axis=-1)  15.3 us
    dot_general x12, matrix products, attend_block(): jnp.einsum('tgqd,rgd->tgqr', queries, keys, preferred_element_type=jnp.fl...  13 us
  transfers between devices with their start and end apart: 4, of which 3 were waited for; matrix products, arithmetic and copies ran while one was open for 28% of the time, Pallas kernels for 0%

commit v1 on v0

--- a/solution.py
+++ b/solution.py
@@ -12,6 +12,12 @@
 EPSILON = 1e-05
 NEG_FILL = -1e30
 FAR_LIMIT = 1 << 30
+
+
+def view_turn(frame_in, which_dim):
+    t_next = jnp.stack([frame_in for _ in range(jax.lax.axis_size("shard"))])
+    f_next = jnp.concatenate(jax.lax.all_to_all(t_next, "shard", 0, 0), axis=which_dim)
+    return f_next
 
 
 def rms_scale(values, gain):
@@ -108,7 +114,7 @@
     new_kv = jnp.concatenate([new_keys.reshape(tok_rows, KVH * HD), new_values], axis=1)
     cache_local = kv_cache[0]
     query_heads = queries.reshape(tok_rows, KVH, groups, HD)
-    piece = lax.all_gather(cache_local, "shard", axis=0, tiled=True)
+    piece = view_turn(cache_local, 0)
     key_pos = jnp.arange(piece.shape[0], dtype=jnp.int32)
     state = fold_rows(empty_state(tok_rows), query_heads, positions, piece, key_pos, length)
     piece = lax.all_gather(new_kv, "shard", axis=0, tiled=True)

time: 384 us -> 474 us (1.23)
  other arithmetic: 48.2 us -> 72.3 us
  waiting for transfers between devices: 153 us -> 177 us
  matrix products: 60.4 us -> 83.1 us
  starting transfers between devices: 5.34 us -> 13.4 us
  local copies, waits for them, and re-layouts: 49.9 us -> 57.6 us
    all_to_all x0 -> x1, waiting for transfers between devices: none -> 132 us  [view_turn(): jax.lax.all_to_all(t_next, 'shard', 0, 0)]
    all_gather x1, waiting for transfers between devices: 55.6 us -> 0.01 us  [local(): weights = lax.all_gather(weights, 'shard', axis=1, tiled=True)]
    all_gather x1 -> x0, waiting for transfers between devices: 51.2 us -> none  [local(): piece = lax.all_gather(cache_local, 'shard', axis=0, tiled=True)]
    reduce_sum x12, other arithmetic: 15.3 us -> 40.4 us  [attend_block(): total = total * factor + jnp.sum(weights, axis=-1)]
    dot_general x12, matrix products: 13 us -> 35.4 us  [attend_block(): jnp.einsum('tgqd,rgd->tgqr', queries, keys, preferred_element_type=jnp.fl...]
    all_to_all x0 -> x1, starting transfers between devices: none -> 7.77 us  [view_turn(): jax.lax.all_to_all(t_next, 'shard', 0, 0)]
    while x60 -> x76, local copies, waits for them, and re-layouts: 10.8 us -> 14.3 us
  transfers between devices with their start and end apart: 4 -> 4, of which waited for: 3 -> 2; matrix products, arithmetic and copies ran while one was open for 28% -> 32% of each run, Pallas kernels for 0% -> 0%
where the time goes in v1:
time: 474 us; the launch traced here: 473 us
  waiting for transfers between devices  177 us (37%)
  matrix products  83.1 us (18%)
  other arithmetic  72.3 us (15%)
  local copies, waits for them, and re-layouts  57.6 us (12%)
  blocking collectives  54.3 us (11%)
  between operations  14.4 us (3%)
  starting transfers between devices  13.4 us (3%)
    all_to_all x1, waiting for transfers between devices, view_turn(): jax.lax.all_to_all(t_next, 'shard', 0, 0)  132 us
    all_to_all x1, blocking collectives, local(): lax.all_to_all(outgoing, 'req', split_axis=0, concat_axis=0, tiled=True)  54.3 us
    all_to_all x1, waiting for transfers between devices, local(): lax.all_to_all(summed.astype(jnp.bfloat16), 'req', split_axis=0, concat_a...  45.4 us
    reduce_sum x12, other arithmetic, attend_block(): total = total * factor + jnp.sum(weights, axis=-1)  40.4 us
    dot_general x12, matrix products, attend_block(): jnp.einsum('tgqd,rgd->tgqr', queries, keys, preferred_element_type=jnp.fl...  35.4 us
    dynamic_slice x24, local copies, waits for them, and re-layouts, fold_rows(): state, _ = lax.scan(advance, state, (blocks, positions))  22.4 us
    dot_general x12, matrix products, attend_block(): jnp.einsum('tgqr,rgd->tgqd', weights.astype(jnp.bfloat16), values, prefer...  17.5 us
    while x76, local copies, waits for them, and re-layouts  14.3 us
  transfers between devices with their start and end apart: 4, of which 2 were waited for; matrix products, arithmetic and copies ran while one was open for 32% of the time, Pallas kernels for 0%

profile of v1, /device:TPU:1, one launch (start us, length us, event | category | flops | bytes accessed | tf_op | source)
XLA Modules:
  0.0 473.1 jit_solution(8992146433690560215)
XLA Ops:
  7.8 4.7 fusion.60
  14.4 4.3 stack.3
  18.8 7.8 %all-to-all-start = ((bf16[16,256,1024]{2,1,0:T(8,128)(2,1)}), bf16[16,256,1024]{2,1,0:T(8,128)(2,1)}, u32[]{:S(2)}, u32[]{:S(2)}) async-start(bf16[16,256,1024]{2,1,0:T(8,128)(2,1)} %stack.3), calls=%async_computation | async-start | bytes 16777216 | tf_op jit(solution)/shard_map/all_to_all | solution.py:19
  28.7 11.3 %reduce-window.6 = s32[40,8,128]{2,1,0:T(8,128)S(1)} reduce-window(s32[40,8,128]{2,1,0:T(8,128)S(1)} %fusion.67, s32[]{:T(128)} %copy.121), window={size=1x1x128 pad=0_0x0_0x127_0}, to_apply=%region_13.14 | reduce-window | flops 5201920 | bytes 327684 | tf_op jit(solution)/shard_map/reduce-window
  42.5 131.8 %all-to-all-done = bf16[16,256,1024]{2,1,0:T(8,128)(2,1)} async-done(((bf16[16,256,1024]{2,1,0:T(8,128)(2,1)}), bf16[16,256,1024]{2,1,0:T(8,128)(2,1)}, u32[]{:S(2)}, u32[]{:S(2)}) %all-to-all-start) | async-done | bytes 8388640 | tf_op jit(solution)/shard_map/all_to_all | solution.py:19
  174.3 111.8 %while.31 = (s32[]{:T(128)}, f32[128,8,3]{0,2,1:T(4,128)S(1)}, f32[128,8,3]{0,2,1:T(4,128)S(1)}, f32[128,8,3,64]{0,3,2,1:T(8,128)}, s32[8,512]{1,0:T(8,128)S(1)}...) while((s32[]{:T(128)}, f32[128,8,3]{0,2,1:T(4,128)S(1)}, ...), condition=%wide.region_4.5_spmd.clone, body=%wide.region_1.4_spmd.clone.sunk | while | flops 420691584 | bytes 60104932 | solution.py:82
  180.9 4.2 fusion.117
  194.5 5.1 %fusion.117 = f32[128,8,3]{0,2,1:T(4,128)S(1)} fusion(f32[8,512,128,3]{2,1,3,0:T(8,128)} %get-tuple-element.405, f32[128,8,3]{0,2,1:T(4,128)S(1)} %select_maximum_fusion.2, pred[128,512]{0,1:T(8,128)(4,1)S(1)} %compare_and_fusion.5), kind=kLoop, calls=%fused_computation.29.clone.1 | loop fusion | flops 6288384 | bytes 6381568 | tf_op jit(solution)/shard_map/while/body/eval_jaxpr/reduce_sum | solution.py:65
  209.6 4.4 fusion.117
  223.4 4.2 fusion.117
  233.2 4.5 fusion.116
  237.8 4.2 fusion.117
  251.4 4.3 fusion.117
  265.3 4.2 fusion.117
  279.0 4.4 fusion.117
  286.1 28.1 %while.30 = (s32[]{:T(128)}, f32[128,8,3]{0,2,1:T(4,128)S(1)}, f32[128,8,3]{0,2,1:T(4,128)S(1)}, f32[128,8,3,64]{0,3,2,1:T(8,128)}, s32[4,512]{1,0:T(4,128)S(1)}...) while((s32[]{:T(128)}, f32[128,8,3]{0,2,1:T(4,128)S(1)}, ...), condition=%wide.region_8.9_spmd.clone, body=%wide.region_5.8_spmd.clone.sunk | while | flops 420485760 | bytes 34939048 | solution.py:82
  320.0 54.3 %all_to_all.15 = bf16[8,5,32,1536]{3,2,1,0:T(8,128)(2,1)} all-to-all(bf16[8,5,32,1536]{3,2,1,0:T(8,128)(2,1)S(1)} %bitcast.210), channel_id=1, replica_groups=mesh['req'=8,'shard'=16] {'req'}, dimensions={0} | all-to-all | bytes 7864320 | tf_op jit(solution)/shard_map/all_to_all | solution.py:151
  374.3 8.1 %fusion.38 = f32[5,512,8,32]{1,3,2,0:T(8,128)} fusion(bf16[5,512,4608]{2,1,0:T(8,128)(2,1)} %all-gather.5.cloned.1.call-done, bf16[8,5,32,1536]{3,2,1,0:T(8,128)(2,1)} %all_to_all.15), kind=kOutput, calls=%fused_computation.49 | convolution fusion | flops 2013265920 | bytes 14417920 | tf_op jit(solution)/shard_map/sjcd,jhd->sjch/dot_general | solution.py:157
  382.4 12.6 %fusion.43 = bf16[8,5,32,1536]{3,2,0,1:T(8,128)(2,1)} fusion(bf16[5,512,4608]{2,1,0:T(8,128)(2,1)} %all-gather.5.cloned.1.call-done, f32[5,512,8,32]{1,3,2,0:T(8,128)} %fusion.38, bf16[8,5,32,1536]{3,2,1,0:T(8,128)(2,1)} %all_to_all.15), kind=kOutput, calls=%fused_computation.58 | convolution fusion | flops 4032430080 | bytes 26214400 | tf_op jit(solution)/shard_map/sjch,jhd->sjcd/dot_general | solution.py:160
  394.9 4.5 copy.70
  399.4 5.4 %all-to-all-start.2 = ((bf16[8,5,32,1536]{3,2,1,0:T(8,128)(2,1)}), bf16[8,5,32,1536]{3,2,1,0:T(8,128)(2,1)}, u32[]{:S(2)}, u32[]{:S(2)}) async-start(bf16[8,5,32,1536]{3,2,1,0:T(8,128)(2,1)} %copy.70), calls=%async_computation.2 | async-start | bytes 7864320 | tf_op jit(solution)/shard_map/all_to_all | solution.py:161
  405.5 45.4 %all-to-all-done.2 = bf16[8,5,32,1536]{3,2,1,0:T(8,128)(2,1)} async-done(((bf16[8,5,32,1536]{3,2,1,0:T(8,128)(2,1)}), bf16[8,5,32,1536]{3,2,1,0:T(8,128)(2,1)}, u32[]{:S(2)}, u32[]{:S(2)}) %all-to-all-start.2) | async-done | bytes 3932192 | tf_op jit(solution)/shard_map/all_to_all | solution.py:161
  450.8 9.9 %gather_fusion = bf16[1024,1536]{1,0:T(8,128)(2,1)} fusion(bf16[1280,1536]{1,0:T(8,128)(2,1)} %bitcast.22, s32[1024]{0:T(1024)S(1)} %broadcast_clamp_fusion), kind=kCustom, calls=%fused_computation | custom fusion | bytes 6295552 | tf_op jit(solution)/shard_map/gather | solution.py:165
  460.7 4.7 fusion.40
  (271 shorter events, 113.6 us)
Async XLA Ops:
  6.5 398.4 %copy-start = (bf16[1536,40]{0,1:T(8,128)(2,1)S(1)}, bf16[1536,40]{0,1:T(8,128)(2,1)}, u32[]{:S(2)}) copy-start(bf16[1536,40]{0,1:T(8,128)(2,1)} %param.23) | copy-start | bytes 368644
  6.5 279.6 %all-gather.3.cloned.1.call-start = ((), (), s32[]{:S(2)}) async-start(), calls=%async_computation.3 | async-start | bytes 4456448 | tf_op jit(solution)/shard_map/all_gather | solution.py:120
  7.8 6.7 %copy-start.7 = (bf16[1,256,1024]{2,1,0:T(8,128)(2,1)S(1)}, bf16[1,256,1024]{2,1,0:T(8,128)(2,1)}, u32[]{:S(2)}) copy-start(bf16[1,256,1024]{2,1,0:T(8,128)(2,1)} %param.20) | copy-start | bytes 1572868
  18.8 8.0 %copy-start.8 = (bf16[5,32,1536]{2,1,0:T(8,128)(2,1)S(1)}, bf16[5,32,1536]{2,1,0:T(8,128)(2,1)}, u32[]{:S(2)}) copy-start(bf16[5,32,1536]{2,1,0:T(8,128)(2,1)} %param.27) | copy-start | bytes 1474564
  18.8 8.0 %copy-start.9 = (bf16[5,32,1536]{2,1,0:T(8,128)(2,1)S(1)}, bf16[5,32,1536]{2,1,0:T(8,128)(2,1)}, u32[]{:S(2)}) copy-start(bf16[5,32,1536]{2,1,0:T(8,128)(2,1)} %param.26) | copy-start | bytes 1474564
  18.8 8.0 %copy-start.10 = (bf16[5,32,1536]{2,1,0:T(8,128)(2,1)S(1)}, bf16[5,32,1536]{2,1,0:T(8,128)(2,1)}, u32[]{:S(2)}) copy-start(bf16[5,32,1536]{2,1,0:T(8,128)(2,1)} %param.25) | copy-start | bytes 1474564
  18.8 9.4 %copy-start.12 = (s32[128,8]{0,1:T(8,128)S(1)}, s32[128,8]{0,1:T(8,128)}, u32[]{:S(2)}) copy-start(s32[128,8]{0,1:T(8,128)} %param.24) | copy-start | bytes 12292
  18.8 155.5 %all-to-all-start = ((bf16[16,256,1024]{2,1,0:T(8,128)(2,1)}), bf16[16,256,1024]{2,1,0:T(8,128)(2,1)}, u32[]{:S(2)}, u32[]{:S(2)}) async-start(bf16[16,256,1024]{2,1,0:T(8,128)(2,1)} %stack.3), calls=%async_computation | async-start | bytes 16777216 | tf_op jit(solution)/shard_map/all_to_all | solution.py:19
  26.6 347.7 %all-gather.5.cloned.1.call-start = ((), (), s32[]{:S(2)}) async-start(), calls=%async_computation.4 | async-start | bytes 25067520 | tf_op jit(solution)/shard_map/all_gather | solution.py:153
  177.1 8.1 %copy-start.3 = (f32[128,8,3,64]{0,3,2,1:T(8,128)S(1)}, f32[128,8,3,64]{0,3,2,1:T(8,128)}, u32[]{:S(2)}) copy-start(f32[128,8,3,64]{0,3,2,1:T(8,128)} %get-tuple-element.423) | copy-start | bytes 2359300 | tf_op jit(solution)/shard_map/while
  190.7 9.0 %copy-start.3 = (f32[128,8,3,64]{0,3,2,1:T(8,128)S(1)}, f32[128,8,3,64]{0,3,2,1:T(8,128)}, u32[]{:S(2)}) copy-start(f32[128,8,3,64]{0,3,2,1:T(8,128)} %get-tuple-element.423) | copy-start | bytes 2359300 | tf_op jit(solution)/shard_map/while
  194.5 6.1 %copy-start.1 = (f32[8,512,128,3]{2,1,3,0:T(8,128)S(1)}, f32[8,512,128,3]{2,1,3,0:T(8,128)}, u32[]{:S(2)}) copy-start(f32[8,512,128,3]{2,1,3,0:T(8,128)} %get-tuple-element.405) | copy-start | bytes 18874372 | tf_op jit(solution)/shard_map/while
  205.8 8.2 %copy-start.3 = (f32[128,8,3,64]{0,3,2,1:T(8,128)S(1)}, f32[128,8,3,64]{0,3,2,1:T(8,128)}, u32[]{:S(2)}) copy-start(f32[128,8,3,64]{0,3,2,1:T(8,128)} %get-tuple-element.423) | copy-start | bytes 2359300 | tf_op jit(solution)/shard_map/while
  209.6 4.8 %copy-start.1 = (f32[8,512,128,3]{2,1,3,0:T(8,128)S(1)}, f32[8,512,128,3]{2,1,3,0:T(8,128)}, u32[]{:S(2)}) copy-start(f32[8,512,128,3]{2,1,3,0:T(8,128)} %get-tuple-element.405) | copy-start | bytes 18874372 | tf_op jit(solution)/shard_map/while
  219.6 8.1 %copy-start.3 = (f32[128,8,3,64]{0,3,2,1:T(8,128)S(1)}, f32[128,8,3,64]{0,3,2,1:T(8,128)}, u32[]{:S(2)}) copy-start(f32[128,8,3,64]{0,3,2,1:T(8,128)} %get-tuple-element.423) | copy-start | bytes 2359300 | tf_op jit(solution)/shard_map/while
  233.2 8.8 %copy-start.3 = (f32[128,8,3,64]{0,3,2,1:T(8,128)S(1)}, f32[128,8,3,64]{0,3,2,1:T(8,128)}, u32[]{:S(2)}) copy-start(f32[128,8,3,64]{0,3,2,1:T(8,128)} %get-tuple-element.423) | copy-start | bytes 2359300 | tf_op jit(solution)/shard_map/while
  247.6 8.2 %copy-start.3 = (f32[128,8,3,64]{0,3,2,1:T(8,128)S(1)}, f32[128,8,3,64]{0,3,2,1:T(8,128)}, u32[]{:S(2)}) copy-start(f32[128,8,3,64]{0,3,2,1:T(8,128)} %get-tuple-element.423) | copy-start | bytes 2359300 | tf_op jit(solution)/shard_map/while
  251.4 4.9 %copy-start.1 = (f32[8,512,128,3]{2,1,3,0:T(8,128)S(1)}, f32[8,512,128,3]{2,1,3,0:T(8,128)}, u32[]{:S(2)}) copy-start(f32[8,512,128,3]{2,1,3,0:T(8,128)} %get-tuple-element.405) | copy-start | bytes 18874372 | tf_op jit(solution)/shard_map/while
  261.5 8.1 %copy-start.3 = (f32[128,8,3,64]{0,3,2,1:T(8,128)S(1)}, f32[128,8,3,64]{0,3,2,1:T(8,128)}, u32[]{:S(2)}) copy-start(f32[128,8,3,64]{0,3,2,1:T(8,128)} %get-tuple-element.423) | copy-start | bytes 2359300 | tf_op jit(solution)/shard_map/while
  265.3 4.7 copy-start.1
  275.1 8.3 %copy-start.3 = (f32[128,8,3,64]{0,3,2,1:T(8,128)S(1)}, f32[128,8,3,64]{0,3,2,1:T(8,128)}, u32[]{:S(2)}) copy-start(f32[128,8,3,64]{0,3,2,1:T(8,128)} %get-tuple-element.423) | copy-start | bytes 2359300 | tf_op jit(solution)/shard_map/while
  279.0 4.8 %copy-start.1 = (f32[8,512,128,3]{2,1,3,0:T(8,128)S(1)}, f32[8,512,128,3]{2,1,3,0:T(8,128)}, u32[]{:S(2)}) copy-start(f32[8,512,128,3]{2,1,3,0:T(8,128)} %get-tuple-element.405) | copy-start | bytes 18874372 | tf_op jit(solution)/shard_map/while
  286.1 29.4 %copy-start.2 = (bf16[128,1536]{1,0:T(8,128)(2,1)S(1)}, bf16[128,1536]{1,0:T(8,128)(2,1)}, u32[]{:S(2)}) copy-start(bf16[128,1536]{1,0:T(8,128)(2,1)} %param.16) | copy-start | bytes 1179652
  399.4 51.4 %all-to-all-start.2 = ((bf16[8,5,32,1536]{3,2,1,0:T(8,128)(2,1)}), bf16[8,5,32,1536]{3,2,1,0:T(8,128)(2,1)}, u32[]{:S(2)}, u32[]{:S(2)}) async-start(bf16[8,5,32,1536]{3,2,1,0:T(8,128)(2,1)} %copy.70), calls=%async_computation.2 | async-start | bytes 7864320 | tf_op jit(solution)/shard_map/all_to_all | solution.py:161
  (20 other events, 39.0 us)
Sparse Core Ops, SparseCore 0:
  14.5 166.4 all-gather.2
  183.2 148.4 all-gather.4
